TPU v7x, 32 devices: a whole 2x2x4 slice. The times are simulated.
32 devices in a mesh: dp: 8 (over z, x), tensor: 4 (over y, core).
Axes of the slice: x: 2, y: 2, z: 4, core: 2. Of those that a mesh axis runs over, the one named last changes fastest.
Arguments:
- hidden: bfloat16 [16384, 1024], P('dp'), may hold values from -6 to 6
- lengths: int32 [8], P('dp'), may hold values from 1365 to 2048, as said below
- norm_gain: float32 [1024], replicated, may hold values from 0.1 to 1.9
- z_weight: bfloat16 [1024, 2048], P(None, 'tensor'), may hold values from -0.1875 to 0.1875
- x_weight: bfloat16 [1024, 2048], P(None, 'tensor'), may hold values from -0.1875 to 0.1875
- bc_weight: bfloat16 [1024, 256], replicated, may hold values from -0.1875 to 0.1875
- dt_weight: bfloat16 [1024, 32], P(None, 'tensor'), may hold values from -0.1875 to 0.1875
- x_kernel: float32 [4, 2048], P(None, 'tensor'), may hold values from -3 to 3
- bc_kernel: float32 [4, 256], replicated, may hold values from -3 to 3
- x_offset: float32 [2048], P('tensor'), may hold values from -3 to 3
- bc_offset: float32 [256], replicated, may hold values from -3 to 3
- step_bias: float32 [32], P('tensor'), may hold values from -5 to -1
- decay_log: float32 [32], P('tensor'), may hold values from 0 to 2.5
- skip_gain: float32 [32], P('tensor'), may hold values from 0.5 to 1.5
- gate_gain: float32 [2048], P('tensor'), may hold values from 0.1 to 1.9
- out_weight: bfloat16 [2048, 1024], P('tensor'), may hold values from -0.125 to 0.125
- cotangent: bfloat16 [16384, 1024], P('dp'), may hold values from -6 to 6
Outputs:
- output: bfloat16 [16384, 1024], P('dp')
- grad_hidden: float32 [16384, 1024], P('dp')
- grad_norm_gain: float32 [1024], replicated
- grad_z_weight: float32 [1024, 2048], P(None, 'tensor')
- grad_x_weight: float32 [1024, 2048], P(None, 'tensor')
- grad_bc_weight: float32 [1024, 256], replicated
- grad_dt_weight: float32 [1024, 32], P(None, 'tensor')
- grad_x_kernel: float32 [4, 2048], P(None, 'tensor')
- grad_bc_kernel: float32 [4, 256], replicated
- grad_x_offset: float32 [2048], P('tensor')
- grad_bc_offset: float32 [256], replicated
- grad_step_bias: float32 [32], P('tensor')
- grad_decay_log: float32 [32], P('tensor')
- grad_skip_gain: float32 [32], P('tensor')
- grad_gate_gain: float32 [2048], P('tensor')
- grad_out_weight: float32 [2048, 1024], P('tensor')
Inputs may be any that keep to these rules, and one draw needn't show every extreme that they name: `lengths`: each slot's sequence length; some slot has exactly 2048 in every draw.
All inputs are finite; a program needn't handle non-finite values.
Results may differ from a plain program's by a relative error of at most 0.0096.
Values may be sent and summed in bfloat16 or wider, within the bound.
No kernel may reach another device: no remote copies, remote signals or barrier semaphores. Data moves between devices by JAX's collectives and lax.ppermute only.
A program may use at most 192 MiB of HBM per device.

v0:
```python
import jax
import jax.numpy as jnp
from jax import lax
from jax.sharding import PartitionSpec as P

CH = 256
DI = 2048
precise = lax.Precision.HIGHEST
epsilon = 1e-05


def causal_conv(signal, kernel, offset):
    taps = kernel.shape[0]
    length = signal.shape[0]
    padded = jnp.pad(signal, ((taps - 1, 0), (0, 0)))
    total = jnp.zeros_like(signal) + offset[None, :]
    for tap_index in range(taps):
        total = total + kernel[tap_index][None, :] * padded[tap_index : tap_index + length]
    return total


def conv_act(signal, kernel, offset):
    return jax.nn.silu(causal_conv(signal, kernel, offset))


def group_step(carry_state, block_in):
    values, log_rates, b_rows, c_rows = block_in
    block_len = log_rates.shape[1]
    causal_mask = lax.broadcasted_iota(
        jnp.int32, (block_len, block_len), 0
    ) >= lax.broadcasted_iota(jnp.int32, (block_len, block_len), 1)
    summed = jnp.cumsum(log_rates, axis=1)
    spread = summed[:, :, None] - summed[:, None, :]
    decays = jnp.exp(jnp.where(causal_mask[None], spread, -1e30))
    scores = jnp.dot(c_rows, b_rows.T, precision=precise, preferred_element_type=jnp.float32)
    within = jnp.einsum("hts,hsp->htp", scores[None] * decays, values, precision=precise)
    carried = (
        jnp.einsum("tn,hnp->htp", c_rows, carry_state, precision=precise)
        * jnp.exp(summed)[:, :, None]
    )
    remain = jnp.exp(summed[:, -1:] - summed)
    updated = carry_state * jnp.exp(summed[:, -1])[:, None, None] + jnp.einsum(
        "sn,hsp->hnp", b_rows, values * remain[:, :, None], precision=precise
    )
    return (updated, within + carried)


def mixer(conv_vals, state_vals, step_raw, step_bias, decay_log, skip_gain, live_mask):
    row_count, channels = conv_vals.shape
    head_count = step_raw.shape[1]
    head_size = channels // head_count
    state_size = state_vals.shape[1] // 2
    block_count = row_count // CH
    step_size = jax.nn.softplus(step_raw + step_bias[None, :]) * live_mask[:, None]
    log_rates = step_size * (-jnp.exp(decay_log))[None, :]
    heads_view = conv_vals.reshape(row_count, head_count, head_size)
    values = heads_view * step_size[:, :, None]
    values = values.reshape(block_count, CH, head_count, head_size).transpose(0, 2, 1, 3)
    log_rates = log_rates.reshape(block_count, CH, head_count).transpose(0, 2, 1)
    b_rows = state_vals[:, :state_size].reshape(block_count, CH, state_size)
    c_rows = state_vals[:, state_size:].reshape(block_count, CH, state_size)
    start_state = jnp.zeros((head_count, state_size, head_size), jnp.float32)
    unused, results = lax.scan(
        jax.checkpoint(group_step), start_state, (values, log_rates, b_rows, c_rows)
    )
    mixed = results.transpose(0, 2, 1, 3).reshape(row_count, head_count, head_size)
    mixed = mixed + skip_gain[None, :, None] * heads_view
    return mixed.reshape(row_count, channels)


def gram(left, right):
    return lax.dot_general(
        left, right, (((0,), (0,)), ((), ())), preferred_element_type=jnp.float32
    )


def back_proj(grad_rows, weight):
    return lax.dot_general(
        grad_rows, weight, (((1,), (1,)), ((), ())), preferred_element_type=jnp.float32
    )


def rounded(value):
    return lax.optimization_barrier(value.astype(jnp.bfloat16)).astype(jnp.float32)


def body(
    hidden,
    lengths,
    norm_gain,
    z_weight,
    x_weight,
    bc_weight,
    dt_weight,
    x_kernel,
    bc_kernel,
    x_offset,
    bc_offset,
    step_bias,
    decay_log,
    skip_gain,
    gate_gain,
    out_weight,
    cotangent,
):
    row_count, model_width = hidden.shape
    parts = lax.axis_size("tensor")
    share = row_count // parts
    start = lax.axis_index("tensor") * share
    inputs = hidden.astype(jnp.float32)
    grad_out = cotangent.astype(jnp.float32)
    live_mask = (lax.iota(jnp.int32, row_count) < lengths[0]).astype(jnp.float32)
    scale = lax.rsqrt(jnp.mean(inputs * inputs, axis=1, keepdims=True) + epsilon)
    normed = (inputs * scale * norm_gain[None, :]).astype(jnp.bfloat16)
    gate_pre = jnp.dot(normed, z_weight, preferred_element_type=jnp.float32)
    conv_in = jnp.dot(normed, x_weight, preferred_element_type=jnp.float32)
    state_in = jnp.dot(normed, bc_weight, preferred_element_type=jnp.float32)
    step_raw = jnp.dot(normed, dt_weight, preferred_element_type=jnp.float32)
    conv_out, conv_pull = jax.vjp(conv_act, conv_in, x_kernel, x_offset)
    state_out, state_pull = jax.vjp(conv_act, state_in, bc_kernel, bc_offset)
    conv_low = rounded(conv_out)
    state_low = rounded(state_out)

    def local_mixer(conv_vals, state_vals, raw_steps, bias_steps, decay_logs, skip_gains):
        return mixer(
            conv_vals, state_vals, raw_steps, bias_steps, decay_logs, skip_gains, live_mask
        )

    mixed_out, mixer_pull = jax.vjp(
        local_mixer, conv_low, state_low, step_raw, step_bias, decay_log, skip_gain
    )
    sigmoid_gate = jax.nn.sigmoid(gate_pre)
    silu_gate = gate_pre * sigmoid_gate
    gated = mixed_out * silu_gate
    squares = lax.psum(jnp.sum(gated * gated, axis=1), "tensor")
    inv_norm = lax.rsqrt(squares / DI + epsilon)[:, None]
    unit_rows = gated * inv_norm
    branch_in = (unit_rows * gate_gain[None, :] * live_mask[:, None]).astype(jnp.bfloat16)
    own_inputs = lax.dynamic_slice_in_dim(inputs, start, share, 0)
    own_scale = lax.dynamic_slice_in_dim(scale, start, share, 0)
    branch = lax.psum(jnp.dot(branch_in, out_weight, preferred_element_type=jnp.float32), "tensor")
    output = (inputs + branch).astype(jnp.bfloat16)
    grad_out_weight = gram(branch_in, cotangent)
    grad_branch = back_proj(cotangent, out_weight) * live_mask[:, None]
    grad_gate_gain = jnp.sum(grad_branch * unit_rows, axis=0)
    grad_unit = grad_branch * gate_gain[None, :]
    cross = lax.psum(jnp.sum(grad_unit * unit_rows, axis=1), "tensor")
    grad_gated = inv_norm * (grad_unit - unit_rows * (cross / DI)[:, None])
    grad_mixed = grad_gated * silu_gate
    grad_gate_pre = grad_gated * mixed_out * sigmoid_gate * (1.0 + gate_pre * (1.0 - sigmoid_gate))
    (
        grad_conv_low,
        grad_state_part,
        grad_step_raw,
        grad_step_bias,
        grad_decay_log,
        grad_skip_gain,
    ) = mixer_pull(grad_mixed)
    grad_state_low = lax.psum(grad_state_part, "tensor")
    grad_conv_in, grad_x_kernel, grad_x_offset = conv_pull(grad_conv_low)
    grad_state_in, grad_bc_kernel, grad_bc_offset = state_pull(grad_state_low)
    low_gate = grad_gate_pre.astype(jnp.bfloat16)
    low_conv = grad_conv_in.astype(jnp.bfloat16)
    low_step = grad_step_raw.astype(jnp.bfloat16)
    low_state = lax.dynamic_slice_in_dim(grad_state_in, start, share, 0).astype(jnp.bfloat16)
    own_normed = lax.dynamic_slice_in_dim(normed, start, share, 0)
    grad_z_weight = gram(normed, low_gate)
    grad_x_weight = gram(normed, low_conv)
    grad_dt_weight = gram(normed, low_step)
    grad_bc_weight = gram(own_normed, low_state)
    state_back = back_proj(low_state, bc_weight)
    grad_normed = (
        back_proj(low_gate, z_weight)
        + back_proj(low_conv, x_weight)
        + back_proj(low_step, dt_weight)
    )
    own_part = lax.dynamic_slice_in_dim(grad_normed, start, share, 0) + state_back
    grad_normed = lax.dynamic_update_slice_in_dim(grad_normed, own_part, start, 0)
    grad_normed = lax.psum(grad_normed, "tensor")
    weighted = grad_normed * norm_gain[None, :]
    row_dots = jnp.sum(weighted * inputs, axis=1, keepdims=True)
    grad_hidden = (
        grad_out + scale * weighted - inputs * scale * scale * scale * row_dots / model_width
    )
    own_grad = lax.dynamic_slice_in_dim(grad_normed, start, share, 0)
    grad_norm_gain = jnp.sum(own_grad * own_inputs * own_scale, axis=0)
    (
        grad_z_weight,
        grad_x_weight,
        grad_dt_weight,
        grad_out_weight,
        grad_x_kernel,
        grad_x_offset,
        grad_step_bias,
        grad_decay_log,
        grad_skip_gain,
        grad_gate_gain,
        grad_bc_kernel,
        grad_bc_offset,
    ) = lax.psum(
        (
            grad_z_weight,
            grad_x_weight,
            grad_dt_weight,
            grad_out_weight,
            grad_x_kernel,
            grad_x_offset,
            grad_step_bias,
            grad_decay_log,
            grad_skip_gain,
            grad_gate_gain,
            grad_bc_kernel,
            grad_bc_offset,
        ),
        "dp",
    )
    grad_bc_weight, grad_norm_gain = lax.psum((grad_bc_weight, grad_norm_gain), ("dp", "tensor"))
    return (
        output,
        grad_hidden,
        grad_norm_gain,
        grad_z_weight,
        grad_x_weight,
        grad_bc_weight,
        grad_dt_weight,
        grad_x_kernel,
        grad_bc_kernel,
        grad_x_offset,
        grad_bc_offset,
        grad_step_bias,
        grad_decay_log,
        grad_skip_gain,
        grad_gate_gain,
        grad_out_weight,
    )


def solution(mesh):
    placed = (
        P("dp", None),
        P("dp"),
        P(),
        P(None, "tensor"),
        P(None, "tensor"),
        P(),
        P(None, "tensor"),
        P(None, "tensor"),
        P(),
        P("tensor"),
        P(),
        P("tensor"),
        P("tensor"),
        P("tensor"),
        P("tensor"),
        P("tensor", None),
        P("dp", None),
    )
    return jax.shard_map(
        body,
        mesh=mesh,
        in_specs=placed,
        out_specs=(
            P("dp", None),
            P("dp", None),
            P(),
            P(None, "tensor"),
            P(None, "tensor"),
            P(),
            P(None, "tensor"),
            P(None, "tensor"),
            P(),
            P("tensor"),
            P(),
            P("tensor"),
            P("tensor"),
            P("tensor"),
            P("tensor"),
            P("tensor", None),
        ),
        check_vma=False,
    )
```

profile of v0, /device:TPU:0, one launch (start us, length us, event | category | flops | bytes accessed | tf_op | source)
XLA Modules:
  0.0 1183.8 jit_solution(3214508663125442144)
XLA Ops:
  41.9 111.8 %while.39 = (s32[]{:T(128)}, f32[8,128,64]{1,2,0:T(8,128)}, f32[8,8,256,64]{2,3,1,0:T(8,128)}, f32[8,8,128,64]{2,3,1,0:T(8,128)}, f32[8,8,256]{2,1,0:T(8,128)}, ...) while((s32[]{:T(128)}, f32[8,128,64]{1,2,0:T(8,128)}, ...), condition=%wide.region_4.5_spmd.clone, body=%wide.region_1.4_spmd.clone.sunk | while | flops 908396544 | bytes 5419819 | solution.py:63
  153.7 7.1 copy.92
  160.8 7.5 reshape.567
  168.4 10.3 multiply_reduce_fusion.13
  178.7 8.5 psum.133
  187.3 9.5 multiply_reduce_fusion.5
  196.7 5.8 psum.135
  202.6 11.1 multiply_reduce_fusion.6
  213.7 5.3 copy.84
  219.0 6.1 copy.99
  230.4 202.6 %while.40 = (s32[]{:T(128)}, f32[8,128,64]{1,2,0:T(8,128)S(1)}, f32[8,8,256,64]{2,3,1,0:T(8,128)}, f32[8,8,256]{2,1,0:T(8,128)}, f32[8,256,128]{2,1,0:T(8,128)},...) while((s32[]{:T(128)}, f32[8,128,64]{1,2,0:T(8,128)S(1)}, ...), condition=%wide.region_22.23_spmd.clone, body=%wide.region_10.22_spmd.clone.sunk | while | flops 2122338304 | bytes 16312063 | solution.py:63
  436.6 8.0 fusion.107
  444.6 7.0 copy.93
  451.6 7.6 reshape.568
  461.6 5.4 copy.89
  474.8 7.0 multiply_reduce_fusion.10
  481.8 6.6 broadcast_multiply_fusion
  488.4 8.1 fusion.85
  496.6 5.6 fusion.124
  502.2 5.6 fusion.123
  508.0 10.3 add_add_fusion
  518.4 6.1 multiply_reduce_fusion.17
  530.0 6.7 fusion.126
  543.3 5.9 fusion.125
  550.0 6.6 convert_element_type.48
  559.8 38.5 %all-reduce.22 = (f32[1024,8]{0,1:T(8,128)}, f32[4,512]{1,0:T(4,128)}, f32[4,256]{1,0:T(4,128)}, f32[512]{0:T(512)}, f32[256]{0:T(256)}, /*index=5*/f32[8]{0:T(128)}, f32[8]{0:T(128)}, f32[8]{0:T(128)}, f32[512]{0:T(512)}) all-reduce(f32[1024,8]{0,1:T(8,128)S(1)} %fusion.101, ...), channel_id=1, replica_groups=mesh['dp'=8,'tensor'=4] {'dp'}, use_global_device_ids=true, to_apply=%region_32.33 | all-reduce | flops 12568 | bytes 100544 | tf_op jit(solution)/shard_map/psum | solution.py:200
  598.2 220.3 %all-reduce.36.cloned.1.call-done = (f32[2048,1024]{1,0:T(8,128)}, f32[2048,1024]{1,0:T(8,128)}) async-done(((f32[2048,1024]{1,0:T(8,128)}, f32[2048,1024]{1,0:T(8,128)}), (f32[2048,1024]{1,0:T(8,128)}, f32[2048,1024]{1,0:T(8,128)})) %all-reduce.36.cloned.1.call-update) | async-done | bytes 16777232 | tf_op jit(solution)/shard_map/psum | solution.py:141
  821.0 39.7 %psum.138 = f32[1024]{0:T(1024)} all-reduce(f32[1024]{0:T(1024)S(1)} %multiply_reduce_fusion.18), channel_id=1, replica_groups=mesh['dp'=8,'tensor'=4] {'dp','tensor'}, use_global_device_ids=true, to_apply=%region_28.29 | all-reduce | flops 1024 | bytes 8192 | tf_op jit(solution)/shard_map/psum | solution.py:217
  860.8 6.0 multiply_reduce_fusion.3
  869.1 9.5 multiply_subtract_fusion
  878.6 76.7 %all-reduce.32.cloned.1.call-done = f32[1024,256]{1,0:T(8,128)} async-done(((f32[1024,256]{1,0:T(8,128)}), f32[1024,256]{1,0:T(8,128)}) %all-reduce.32.cloned.1.call-update) | async-done | bytes 1048592 | tf_op jit(solution)/shard_map/psum | solution.py:217
  955.3 214.6 %all-reduce.34.cloned.1.call-done = (f32[1024,512]{1,0:T(8,128)}, f32[1024,512]{1,0:T(8,128)}, f32[512,1024]{1,0:T(8,128)}) async-done(((f32[1024,512]{1,0:T(8,128)}, f32[1024,512]{1,0:T(8,128)}, f32[512,1024]{1,0:T(8,128)}), (f32[1024,512]{1,0:T(8,128)}, f32[1024,512]{1,0:T(8,128)}, f32[512,1024]{1,0:T(8,128)})) %all-reduce.34.cloned.1.call-update) | async-done | bytes 6291472 | tf_op jit(solution)/shard_map/psum | solution.py:200
  (580 shorter events, 394.3 us)
Async XLA Ops:
  7.2 161.2 %copy-start = (bf16[1024,512]{1,0:T(8,128)(2,1)S(1)}, bf16[1024,512]{1,0:T(8,128)(2,1)}, u32[]{:S(2)}) copy-start(bf16[1024,512]{1,0:T(8,128)(2,1)} %param.24) | copy-start | bytes 3145732
  7.2 511.1 %all-reduce.30.cloned.1.call-start = ((), (), s32[]{:S(2)}) async-start(), calls=%async_computation | async-start | bytes 4194304 | tf_op jit(solution)/shard_map/psum | solution.py:159
  160.8 7.5 copy-start.62
  168.4 18.8 %copy-start.34 = (f32[512]{0:T(512)S(1)}, f32[512]{0:T(512)}, u32[]{:S(2)}) copy-start(f32[512]{0:T(512)} %param.35) | copy-start | bytes 6148
  436.1 382.4 %all-reduce.36.cloned.1.call-start = ((), (), s32[]{:S(2)}) async-start(), calls=%async_computation.3 | async-start | bytes 33554432 | tf_op jit(solution)/shard_map/psum | solution.py:141
  451.6 7.6 copy-start.20
  474.8 7.0 copy-start.36
  474.8 7.0 copy-start.38
  474.8 7.0 copy-start.40
  488.4 8.1 copy-start.64
  496.6 5.6 copy-start.13
  502.2 5.6 copy-start.25
  502.2 5.6 copy-start.26
  502.2 5.6 copy-start.56
  502.2 5.8 copy-start.31
  518.3 6.2 copy-start.42
  518.3 6.2 copy-start.44
  518.3 6.2 copy-start.46
  518.3 6.2 copy-start.48
  529.7 425.6 %all-reduce.32.cloned.1.call-start = ((), (), s32[]{:S(2)}) async-start(), calls=%async_computation.1 | async-start | bytes 2097152 | tf_op jit(solution)/shard_map/psum | solution.py:217
  529.9 6.7 copy-start.8
  530.0 6.7 copy-start.16
  543.3 626.7 %all-reduce.34.cloned.1.call-start = ((), (), s32[]{:S(2)}) async-start(), calls=%async_computation.2 | async-start | bytes 12582912 | tf_op jit(solution)/shard_map/psum | solution.py:200
  550.0 6.6 copy-start.49
  550.0 6.8 copy-start.50
  550.0 6.8 copy-start.51
  550.0 6.8 copy-start.52
  550.0 6.9 copy-start.53
  550.0 6.9 copy-start.66
  556.9 303.9 %copy-start.33 = (f32[1024]{0:T(1024)S(1)}, f32[1024]{0:T(1024)}, u32[]{:S(2)}) copy-start(f32[1024]{0:T(1024)} %param.23) | copy-start | bytes 12292
  860.8 6.0 copy-start.4
  860.8 8.4 copy-start.5
  (39 other events, 134.2 us)
Sparse Core Ops, SparseCore 0:
  436.3 51.7 all-reduce.29
  529.8 288.6 all-reduce.35
  824.3 131.0 all-reduce.31
  960.6 209.3 all-reduce.33
where the time goes:
time: 1190 us; the launch traced here: 1180 us
  waiting for transfers between devices  512 us (43%)
  matrix products  276 us (23%)
  local copies, waits for them, and re-layouts  150 us (13%)
  other arithmetic  136 us (11%)
  blocking collectives  92.5 us (8%)
  between operations  15.4 us (1%)
    psum x1, waiting for transfers between devices, body(): lax.psum(jnp.dot(branch_in, out_weight, preferred_element_type=jnp.float3...  220 us
    psum x1, waiting for transfers between devices, body(): lax.psum((grad_z_weight, grad_x_weight, grad_dt_weight, grad_out_weight,...  215 us
    dot_general x24, matrix products, group_step(): jnp.einsum('hts,hsp->htp', scores[None] * decays, values, precision=precise)  89.6 us
    psum x1, waiting for transfers between devices, body(): lax.psum((grad_bc_weight, grad_norm_gain), ('dp', 'tensor'))  76.7 us
    psum x1, blocking collectives, body(): lax.psum((grad_bc_weight, grad_norm_gain), ('dp', 'tensor'))  39.7 us
    another operation x57, other arithmetic  38.8 us
    psum x1, blocking collectives, body(): lax.psum((grad_z_weight, grad_x_weight, grad_dt_weight, grad_out_weight,...  38.5 us
    dot_general x24, matrix products, group_step(): jnp.einsum('sn,hsp->hnp', b_rows, values * remain[:, :, None], precision=...  37.8 us
  transfers between devices with their start and end apart: 4, of which 3 were waited for; matrix products, arithmetic and copies ran while one was open for 11% of the time, Pallas kernels for 0%

commit v1 on v0

--- a/solution.py
+++ b/solution.py
@@ -138,7 +138,8 @@
     branch_in = (unit_rows * gate_gain[None, :] * live_mask[:, None]).astype(jnp.bfloat16)
     own_inputs = lax.dynamic_slice_in_dim(inputs, start, share, 0)
     own_scale = lax.dynamic_slice_in_dim(scale, start, share, 0)
-    branch = lax.psum(jnp.dot(branch_in, out_weight, preferred_element_type=jnp.float32), "tensor")
+    message = jnp.dot(branch_in, out_weight, preferred_element_type=jnp.float32)
+    branch = jax.lax.all_gather(message, "tensor").sum(axis=0)
     output = (inputs + branch).astype(jnp.bfloat16)
     grad_out_weight = gram(branch_in, cotangent)
     grad_branch = back_proj(cotangent, out_weight) * live_mask[:, None]

time: 1190 us -> 1250 us (1.050)
  waiting for transfers between devices: 512 us -> 550 us
  other arithmetic: 136 us -> 158 us
    all_gather x0 -> x1, waiting for transfers between devices: none -> 155 us  [body(): branch = jax.lax.all_gather(message, 'tensor').sum(axis=0)]
    psum x1, waiting for transfers between devices: 220 us -> 76.3 us  [body(): grad_normed = lax.psum(grad_normed, 'tensor')]
    psum x1, waiting for transfers between devices: 76.7 us -> 105 us  [body(): lax.psum((grad_bc_weight, grad_norm_gain), ('dp', 'tensor'))]
    reduce_sum x0 -> x1, other arithmetic: none -> 16.7 us  [body(): branch = jax.lax.all_gather(message, 'tensor').sum(axis=0)]
    unnamed x141 -> x135, local copies, waits for them, and re-layouts: 29.3 us -> 26.6 us
  transfers between devices with their start and end apart: 4 -> 5, of which waited for: 3 -> 4; matrix products, arithmetic and copies ran while one was open for 11% -> 12% of each run, Pallas kernels for 0% -> 0%
where the time goes in v1:
time: 1250 us; the launch traced here: 1240 us
  waiting for transfers between devices  550 us (44%)
  matrix products  277 us (22%)
  other arithmetic  158 us (13%)
  local copies, waits for them, and re-layouts  148 us (12%)
  blocking collectives  93.4 us (7%)
  between operations  15.6 us (1%)
    psum x1, waiting for transfers between devices, body(): lax.psum((grad_z_weight, grad_x_weight, grad_dt_weight, grad_out_weight,...  215 us
    all_gather x1, waiting for transfers between devices, body(): branch = jax.lax.all_gather(message, 'tensor').sum(axis=0)  155 us
    psum x1, waiting for transfers between devices, body(): lax.psum((grad_bc_weight, grad_norm_gain), ('dp', 'tensor'))  105 us
    dot_general x24, matrix products, group_step(): jnp.einsum('hts,hsp->htp', scores[None] * decays, values, precision=precise)  89.9 us
    psum x1, waiting for transfers between devices, body(): grad_normed = lax.psum(grad_normed, 'tensor')  76.3 us
    psum x1, blocking collectives, body(): lax.psum((grad_bc_weight, grad_norm_gain), ('dp', 'tensor'))  40.3 us
    another operation x57, other arithmetic  38.9 us
    psum x1, blocking collectives, body(): lax.psum((grad_z_weight, grad_x_weight, grad_dt_weight, grad_out_weight,...  38.7 us
  transfers between devices with their start and end apart: 5, of which 4 were waited for; matrix products, arithmetic and copies ran while one was open for 12% of the time, Pallas kernels for 0%

profile of v1, /device:TPU:0, one launch (start us, length us, event | category | flops | bytes accessed | tf_op | source)
XLA Modules:
  0.0 1244.3 jit_solution(1133785539458134213)
XLA Ops:
  41.9 112.0 %while.39 = (s32[]{:T(128)}, f32[8,128,64]{1,2,0:T(8,128)}, f32[8,8,256,64]{2,3,1,0:T(8,128)}, f32[8,8,128,64]{2,3,1,0:T(8,128)}, f32[8,8,256]{2,1,0:T(8,128)}, ...) while((s32[]{:T(128)}, f32[8,128,64]{1,2,0:T(8,128)}, ...), condition=%wide.region_4.5_spmd.clone, body=%wide.region_1.4_spmd.clone.sunk | while | flops 908396544 | bytes 5419819 | solution.py:63
  153.9 7.1 copy.92
  161.0 7.5 reshape.568
  168.6 10.3 multiply_reduce_fusion.13
  179.0 8.5 psum.126
  187.5 9.5 multiply_reduce_fusion.5
  197.0 5.8 psum.127
  202.8 11.1 multiply_reduce_fusion.6
  219.3 6.1 copy.99
  230.6 203.3 %while.40 = (s32[]{:T(128)}, f32[8,128,64]{1,2,0:T(8,128)S(1)}, f32[8,8,256,64]{2,3,1,0:T(8,128)}, f32[8,8,256]{2,1,0:T(8,128)}, f32[8,256,128]{2,1,0:T(8,128)},...) while((s32[]{:T(128)}, f32[8,128,64]{1,2,0:T(8,128)S(1)}, ...), condition=%wide.region_22.23_spmd.clone, body=%wide.region_10.22_spmd.clone.sunk | while | flops 2122338304 | bytes 16312063 | solution.py:63
  437.0 7.1 copy.93
  444.1 7.5 reshape.569
  467.0 7.0 multiply_reduce_fusion.10
  474.0 6.6 broadcast_multiply_fusion
  480.6 8.2 fusion.85
  488.8 5.6 fusion.124
  494.5 5.8 fusion.123
  500.5 10.5 add_add_fusion
  510.9 6.1 multiply_reduce_fusion.17
  522.4 8.2 fusion.107
  530.7 6.7 fusion.126
  544.1 5.9 fusion.125
  550.8 6.6 convert_element_type.48
  560.5 38.7 %all-reduce.22 = (f32[1024,8]{0,1:T(8,128)}, f32[4,512]{1,0:T(4,128)}, f32[4,256]{1,0:T(4,128)}, f32[512]{0:T(512)}, f32[256]{0:T(256)}, /*index=5*/f32[8]{0:T(128)}, f32[8]{0:T(128)}, f32[8]{0:T(128)}, f32[512]{0:T(512)}) all-reduce(f32[1024,8]{0,1:T(8,128)S(1)} %fusion.101, ...), channel_id=1, replica_groups=mesh['dp'=8,'tensor'=4] {'dp'}, use_global_device_ids=true, to_apply=%region_32.33 | all-reduce | flops 12568 | bytes 100544 | tf_op jit(solution)/shard_map/psum | solution.py:201
  599.2 76.3 %all-reduce.31.cloned.1.call-done = f32[2048,1024]{1,0:T(8,128)} async-done(((f32[2048,1024]{1,0:T(8,128)}), f32[2048,1024]{1,0:T(8,128)}) %all-reduce.31.cloned.1.call-update) | async-done | bytes 8388624 | tf_op jit(solution)/shard_map/psum | solution.py:180
  678.0 40.3 %psum.130 = f32[1024]{0:T(1024)} all-reduce(f32[1024]{0:T(1024)S(1)} %multiply_reduce_fusion.18), channel_id=1, replica_groups=mesh['dp'=8,'tensor'=4] {'dp','tensor'}, use_global_device_ids=true, to_apply=%region_28.29 | all-reduce | flops 1024 | bytes 8192 | tf_op jit(solution)/shard_map/psum | solution.py:218
  718.3 6.2 multiply_reduce_fusion.3
  724.5 154.9 %all-gather.3.cloned.1.call-done = f32[8192,1024]{1,0:T(8,128)} async-done(((f32[2048,1024]{1,0:T(8,128)}), f32[8192,1024]{1,0:T(8,128)}) %all-gather.3.cloned.1.call-update) | async-done | bytes 33554448 | tf_op jit(solution)/shard_map/all_gather | solution.py:142
  879.4 16.7 %reduce_sum.387 = f32[2048,1024]{1,0:T(8,128)} reduce(f32[4,2048,1024]{2,1,0:T(8,128)} %bitcast.308, f32[]{:T(128)} %constant.134.clone.1), dimensions={0}, to_apply=%region_7.8 | reduce | flops 6291456 | bytes 41943044 | tf_op jit(solution)/shard_map/reduce_sum | solution.py:142
  896.2 15.0 %multiply_subtract_fusion = (f32[2048,1024]{1,0:T(8,128)}, bf16[2048,1024]{1,0:T(8,128)(2,1)}) fusion(bf16[2048,1024]{1,0:T(8,128)(2,1)} %param.37, bf16[2048,1024]{1,0:T(8,128)(2,1)} %param.21, f32[2048,1024]{1,0:T(8,128)} %all-reduce.31.cloned.1.call-done, f32[2048]{0:T(1024)S(1)} %multiply_reduce_fusion.3, f32[1024]{0:T(1024)S(1)} %copy-done.30, ...), kind=kLoop, calls=%fused_computation.108 | loop fusion | flops 27262976 | bytes 37769216 | tf_op jit(solution)/shard_map/sub | solution.py:184
  911.2 104.5 %all-reduce.33.cloned.1.call-done = f32[1024,256]{1,0:T(8,128)} async-done(((f32[1024,256]{1,0:T(8,128)}), f32[1024,256]{1,0:T(8,128)}) %all-reduce.33.cloned.1.call-update) | async-done | bytes 1048592 | tf_op jit(solution)/shard_map/psum | solution.py:218
  1015.7 214.6 %all-reduce.35.cloned.1.call-done = (f32[1024,512]{1,0:T(8,128)}, f32[1024,512]{1,0:T(8,128)}, f32[512,1024]{1,0:T(8,128)}) async-done(((f32[1024,512]{1,0:T(8,128)}, f32[1024,512]{1,0:T(8,128)}, f32[512,1024]{1,0:T(8,128)}), (f32[1024,512]{1,0:T(8,128)}, f32[1024,512]{1,0:T(8,128)}, f32[512,1024]{1,0:T(8,128)})) %all-reduce.35.cloned.1.call-update) | async-done | bytes 6291472 | tf_op jit(solution)/shard_map/psum | solution.py:201
  (578 shorter events, 402.4 us)
Async XLA Ops:
  7.2 161.4 %copy-start = (bf16[1024,512]{1,0:T(8,128)(2,1)S(1)}, bf16[1024,512]{1,0:T(8,128)(2,1)}, u32[]{:S(2)}) copy-start(bf16[1024,512]{1,0:T(8,128)(2,1)} %param.24) | copy-start | bytes 3145732
  7.2 503.7 %all-reduce.29.cloned.1.call-start = ((), (), s32[]{:S(2)}) async-start(), calls=%async_computation | async-start | bytes 4194304 | tf_op jit(solution)/shard_map/psum | solution.py:160
  161.0 7.5 copy-start.59
  168.6 18.9 %copy-start.31 = (f32[512]{0:T(512)S(1)}, f32[512]{0:T(512)}, u32[]{:S(2)}) copy-start(f32[512]{0:T(512)} %param.35) | copy-start | bytes 6148
  437.0 238.5 %all-reduce.31.cloned.1.call-start = ((), (), s32[]{:S(2)}) async-start(), calls=%async_computation.1 | async-start | bytes 16777216 | tf_op jit(solution)/shard_map/psum | solution.py:180
  444.1 7.6 copy-start.18
  467.0 7.0 copy-start.33
  467.0 7.0 copy-start.35
  467.0 7.0 copy-start.37
  480.6 8.2 copy-start.61
  488.8 5.6 copy-start.11
  488.8 5.6 copy-start.10
  494.4 5.8 copy-start.22
  494.4 5.8 copy-start.23
  494.4 5.8 copy-start.53
  494.5 6.0 copy-start.28
  510.9 6.1 copy-start.39
  510.9 6.1 copy-start.41
  510.9 6.1 copy-start.43
  510.9 6.1 copy-start.45
  522.2 357.2 %all-gather.3.cloned.1.call-start = ((), (), s32[]{:S(2)}) async-start(), calls=%async_computation.3 | async-start | bytes 41943040 | tf_op jit(solution)/shard_map/all_gather | solution.py:142
  530.6 485.1 %all-reduce.33.cloned.1.call-start = ((), (), s32[]{:S(2)}) async-start(), calls=%async_computation.2 | async-start | bytes 2097152 | tf_op jit(solution)/shard_map/psum | solution.py:218
  530.7 6.7 copy-start.6
  530.7 6.7 copy-start.14
  544.0 686.3 %all-reduce.35.cloned.1.call-start = ((), (), s32[]{:S(2)}) async-start(), calls=%async_computation.4 | async-start | bytes 12582912 | tf_op jit(solution)/shard_map/psum | solution.py:201
  550.8 6.6 copy-start.46
  550.8 6.8 copy-start.47
  550.8 6.8 copy-start.48
  550.8 6.8 copy-start.49
  550.8 6.8 copy-start.50
  550.8 6.8 copy-start.63
  557.6 160.7 %copy-start.30 = (f32[1024]{0:T(1024)S(1)}, f32[1024]{0:T(1024)}, u32[]{:S(2)}) copy-start(f32[1024]{0:T(1024)} %param.23) | copy-start | bytes 12292
  (37 other events, 124.1 us)
Sparse Core Ops, SparseCore 0:
  437.1 51.7 all-reduce.28
  522.3 153.1 all-reduce.30
  677.0 202.3 all-gather.2
  885.0 130.6 all-reduce.32
  1021.0 209.3 all-reduce.34
